TPU v7x, 512 devices: a whole 4x8x8 slice. The times are simulated.
512 devices in a mesh: ctx: 32 (over z, x), exp: 16 (over y, core).
Axes of the slice: x: 4, y: 8, z: 8, core: 2. Of those that a mesh axis runs over, the one named last changes fastest.
Arguments:
- stream: bfloat16 [16, 4096, 1024], P('exp', 'ctx'), may hold values from -400 to 400
- queries: bfloat16 [16, 4096, 16, 128], P('exp', 'ctx'), may hold values from -6 to 6
- key_rows: bfloat16 [16, 4096, 2, 128], P('exp', 'ctx'), may hold values from -4 to 4
- value_rows: bfloat16 [16, 4096, 2, 128], P('exp', 'ctx'), may hold values from -6 to 6
- expert_ids: int32 [16, 4096, 2], P('exp', 'ctx'), may hold values from 0 to 127, as said below
- norm_gain: bfloat16 [1024], replicated, may hold values from 0.099609375 to 1.8984375
- router_weight: bfloat16 [1024, 128], replicated, may hold values from -0.1875 to 0.1875
- gate_weight: bfloat16 [98304, 1024], P(('ctx', 'exp')), may hold values from -0.1875 to 0.1875
- up_weight: bfloat16 [98304, 1024], P(('ctx', 'exp')), may hold values from -0.1875 to 0.1875
- down_weight: bfloat16 [98304, 1024], P(('ctx', 'exp')), may hold values from -0.21875 to 0.21875
Outputs:
- attended: bfloat16 [16, 4096, 16, 128], P('exp', 'ctx')
- expert_mix: bfloat16 [16, 4096, 1024], P('exp', 'ctx')
Inputs may be any that keep to these rules, and one draw needn't show every extreme that they name: `expert_ids`: within the rows of one device (aligned blocks of 128 positions of one sequence), a token's 2 experts differ and no expert is named more than 4 times; one expert is named exactly 4 times in every such block.
All inputs are finite; a program needn't handle non-finite values.
Results may differ from a plain program's by a relative error of at most 0.01.
Values may be sent and summed in bfloat16 or wider, within the bound.
No kernel may reach another device: no remote copies, remote signals or barrier semaphores. Data moves between devices by JAX's collectives and lax.ppermute only.
A program may use at most 64 MiB of HBM per device.

v0:
```python
import math
import jax
import jax.numpy as jnp
from jax import lax
from jax.sharding import PartitionSpec as P


def from_partner(value, axis, bit):
    return lax.ppermute(value, axis, [(i, i ^ 1 << bit) for i in range(lax.axis_size(axis))])


def expert_rows(inputs, gate_rows, up_rows, down_rows):
    features = inputs.shape[-1]
    flat_rows = inputs.reshape(-1, features)
    contract = (((1,), (1,)), ((), ()))
    gate_part = lax.dot_general(flat_rows, gate_rows, contract, preferred_element_type=jnp.float32)
    up_part = lax.dot_general(flat_rows, up_rows, contract, preferred_element_type=jnp.float32)
    hidden = (jax.nn.silu(gate_part) * up_part).astype(jnp.bfloat16)
    projected = jnp.dot(hidden, down_rows, preferred_element_type=jnp.float32)
    return projected.reshape(inputs.shape)


def attention(queries, key_rows, value_rows):
    seq_rows = queries.shape[1]
    head_count = queries.shape[2]
    head_size = queries.shape[3]
    kv_count = key_rows.shape[2]
    group_size = head_count // kv_count
    grouped = queries[0].reshape(seq_rows, kv_count, group_size, head_size)
    scaling = 1.0 / math.sqrt(head_size)
    query_pos = lax.axis_index("ctx") * seq_rows + jnp.arange(seq_rows, dtype=jnp.int32)
    initial = (
        jnp.full((kv_count, group_size, seq_rows), -1e30, jnp.float32),
        jnp.zeros((kv_count, group_size, seq_rows), jnp.float32),
        jnp.zeros((kv_count, group_size, seq_rows, head_size), jnp.float32),
    )
    key_piece = lax.all_gather(key_rows, "ctx", axis=1, tiled=True)
    value_piece = lax.all_gather(value_rows, "ctx", axis=1, tiled=True)
    piece_rows = key_piece.shape[1]
    block_rows = math.gcd(piece_rows, 512)
    block_count = piece_rows // block_rows
    key_blocks = key_piece[0].reshape(block_count, block_rows, kv_count, head_size)
    value_blocks = value_piece[0].reshape(block_count, block_rows, kv_count, head_size)

    def advance(status, members):
        running, totals, accumulated = status
        key_block, value_block, offset = members
        scores = (
            jnp.einsum("qhgd,khd->hgqk", grouped, key_block, preferred_element_type=jnp.float32)
            * scaling
        )
        key_pos = offset * block_rows + jnp.arange(block_rows, dtype=jnp.int32)
        visible = key_pos[None, :] <= query_pos[:, None]
        scores = jnp.where(visible, scores, -1e30)
        highest = jnp.maximum(running, jnp.max(scores, axis=-1))
        factor = jnp.exp(running - highest)
        weights = jnp.where(visible, jnp.exp(scores - highest[..., None]), 0.0)
        totals = totals * factor + jnp.sum(weights, axis=-1)
        accumulated = accumulated * factor[..., None] + jnp.einsum(
            "hgqk,khd->hgqd",
            weights.astype(jnp.bfloat16),
            value_block,
            preferred_element_type=jnp.float32,
        )
        return ((highest, totals, accumulated), None)

    status, unused = lax.scan(
        advance, initial, (key_blocks, value_blocks, jnp.arange(block_count, dtype=jnp.int32))
    )
    running, totals, accumulated = status
    result = accumulated / totals[..., None]
    return (
        jnp.transpose(result, (2, 0, 1, 3))
        .reshape(1, seq_rows, head_count, head_size)
        .astype(jnp.bfloat16)
    )


def local(
    stream,
    queries,
    key_rows,
    value_rows,
    expert_ids,
    norm_gain,
    router_weight,
    gate_weight,
    up_weight,
    down_weight,
):
    attended = attention(queries, key_rows, value_rows)
    ctx_count = lax.axis_size("ctx")
    exp_count = lax.axis_size("exp")
    tokens = stream.shape[1]
    features = stream.shape[2]
    top_count = expert_ids.shape[2]
    expert_total = router_weight.shape[1]
    per_ctx = expert_total // ctx_count
    quarters = exp_count // per_ctx
    capacity = 2 * tokens * top_count // expert_total
    widened = stream[0].astype(jnp.float32)
    mean_square = jnp.mean(widened * widened, axis=-1, keepdims=True)
    normed = (widened * lax.rsqrt(mean_square + 1e-06) * norm_gain.astype(jnp.float32)).astype(
        jnp.bfloat16
    )
    logits = jnp.dot(normed, router_weight, preferred_element_type=jnp.float32)
    chosen = expert_ids[0]
    gate_values = jax.nn.sigmoid(jnp.take_along_axis(logits, chosen, axis=1))
    flat_ids = chosen.reshape(-1)
    onehot = (flat_ids[:, None] == jnp.arange(expert_total, dtype=jnp.int32)[None, :]).astype(
        jnp.int32
    )
    earlier = jnp.cumsum(onehot, axis=0) - onehot
    slot_index = jnp.sum(earlier * onehot, axis=1)
    target = (flat_ids % per_ctx * ctx_count + flat_ids // per_ctx) * capacity + slot_index
    source_rows = jnp.repeat(normed, top_count, axis=0)
    outgoing = (
        jnp.zeros((expert_total * capacity, features), jnp.bfloat16).at[target].set(source_rows)
    )
    outgoing = outgoing.reshape(per_ctx, ctx_count, capacity, features)
    arrived = lax.all_to_all(outgoing, "ctx", split_axis=1, concat_axis=1, tiled=True)
    stacked = jnp.stack([gate_weight, up_weight, down_weight], axis=0)
    my_exp = lax.axis_index("exp")
    partner = from_partner(stacked, "exp", 0)
    upper_side = my_exp & 1 == 1
    held = jnp.where(
        upper_side,
        jnp.concatenate([partner, stacked], axis=1),
        jnp.concatenate([stacked, partner], axis=1),
    )
    half_ctx = ctx_count // 2
    halves_rows = arrived.reshape(per_ctx, 1, 2, half_ctx, capacity, features)
    spread_rows = jnp.broadcast_to(
        halves_rows, (per_ctx, quarters // 2, 2, half_ctx, capacity, features)
    )
    spread_rows = spread_rows.reshape(exp_count, half_ctx, capacity, features)
    received = lax.all_to_all(spread_rows, "exp", split_axis=0, concat_axis=0, tiled=True)
    partials = expert_rows(received, held[0], held[1], held[2])
    returned = lax.all_to_all(
        partials.astype(jnp.bfloat16), "exp", split_axis=0, concat_axis=0, tiled=True
    ).astype(partials.dtype)
    summed = jnp.sum(
        returned.reshape(per_ctx, quarters // 2, 2, half_ctx, capacity, features), axis=1
    )
    finished = summed.astype(jnp.bfloat16).reshape(per_ctx, ctx_count, capacity, features)
    came_back = lax.all_to_all(finished, "ctx", split_axis=1, concat_axis=1, tiled=True)
    flat_back = came_back.reshape(expert_total * capacity, features)
    picked = (
        jnp.take(flat_back, target, axis=0).astype(jnp.float32).reshape(tokens, top_count, features)
    )
    mixture = jnp.sum(picked * gate_values[:, :, None], axis=1).astype(jnp.bfloat16)
    return (attended, mixture[None])


def solution(mesh):
    placed = (
        P("exp", "ctx", None),
        P("exp", "ctx", None, None),
        P("exp", "ctx", None, None),
        P("exp", "ctx", None, None),
        P("exp", "ctx", None),
        P(),
        P(),
        P(("ctx", "exp"), None),
        P(("ctx", "exp"), None),
        P(("ctx", "exp"), None),
    )
    return jax.shard_map(
        local,
        mesh=mesh,
        in_specs=placed,
        out_specs=(P("exp", "ctx", None, None), P("exp", "ctx", None)),
        check_vma=False,
    )
```

profile of v0, /device:TPU:16, one launch (start us, length us, event | category | flops | bytes accessed | tf_op | source)
XLA Modules:
  0.0 309.8 jit_solution(2212090198150793443)
XLA Ops:
  12.4 1.9 scatter_custom_fusion
  16.4 13.2 %all-to-all-start = ((bf16[4,32,4,1024]{3,2,0,1:T(4,128)(2,1)}), bf16[4,32,4,1024]{3,2,0,1:T(4,128)(2,1)S(1)}, u32[]{:S(2)}, u32[]{:S(2)}) async-start(bf16[4,32,4,1024]{3,2,0,1:T(4,128)(2,1)} %copy.84), calls=%async_computation | async-start | bytes 2097152 | tf_op jit(solution)/shard_map/all_to_all | solution.py:121
  30.3 27.4 %all-to-all-done = bf16[4,32,4,1024]{3,2,0,1:T(4,128)(2,1)S(1)} async-done(((bf16[4,32,4,1024]{3,2,0,1:T(4,128)(2,1)}), bf16[4,32,4,1024]{3,2,0,1:T(4,128)(2,1)S(1)}, u32[]{:S(2)}, u32[]{:S(2)}) %all-to-all-start) | async-done | bytes 1048608 | tf_op jit(solution)/shard_map/all_to_all | solution.py:121
  58.1 2.1 broadcast_in_dim.66
  60.2 7.6 %all-to-all-start.1 = ((bf16[16,16,4,1024]{3,2,1,0:T(4,128)(2,1)}), bf16[16,16,4,1024]{3,2,1,0:T(4,128)(2,1)S(1)}, u32[]{:S(2)}, u32[]{:S(2)}) async-start(bf16[16,16,4,1024]{3,2,1,0:T(4,128)(2,1)} %bitcast.120), calls=%async_computation.1 | async-start | bytes 4194304 | tf_op jit(solution)/shard_map/all_to_all | solution.py:137
  67.8 2.2 pad_maximum_fusion
  70.0 2.0 collective-permute-start
  72.7 2.3 collective-permute-done
  75.1 3.5 %maximum_select_fusion = bf16[3,384,1024]{2,1,0:T(8,128)(2,1)} fusion(bf16[1,192,1024]{2,1,0:T(8,128)(2,1)S(1)} %bitcast.124, bf16[1,192,1024]{2,1,0:T(8,128)(2,1)S(1)} %bitcast.126, bf16[1,192,1024]{2,1,0:T(8,128)(2,1)} %bitcast.128, bf16[3,192,1024]{2,1,0:T(8,128)(2,1)} %collective-permute-done, pred[]{:T(512)S(6)} %eq.35), kind=kLoop, calls=%fused_computation.30 | loop fusion | flops 20054016 | bytes 4718593 | tf_op jit(solution)/shard_map/jit(_where)/select_n | solution.py:126
  78.6 36.6 %all-to-all-done.1 = bf16[16,16,4,1024]{3,2,1,0:T(4,128)(2,1)S(1)} async-done(((bf16[16,16,4,1024]{3,2,1,0:T(4,128)(2,1)}), bf16[16,16,4,1024]{3,2,1,0:T(4,128)(2,1)S(1)}, u32[]{:S(2)}, u32[]{:S(2)}) %all-to-all-start.1) | async-done | bytes 2097184 | tf_op jit(solution)/shard_map/all_to_all | solution.py:137
  115.2 2.0 reshape.284
  117.2 3.2 %fusion.22 = f32[1024,384]{1,0:T(8,128)S(1)} fusion(bf16[1024,1024]{1,0:T(8,128)(2,1)} %reshape.284, bf16[3,384,1024]{2,1,0:T(8,128)(2,1)} %maximum_select_fusion), kind=kOutput, calls=%fused_computation.40 | convolution fusion | flops 805306368 | bytes 4456448 | tf_op jit(solution)/shard_map/dot_general | solution.py:16
  120.4 2.3 multiply_convert_fusion
  122.7 2.4 dot_general.22
  125.1 3.7 %convolution_convert_fusion = bf16[16,16,4,1024]{3,1,2,0:T(8,128)(2,1)} fusion(bf16[3,384,1024]{2,1,0:T(8,128)(2,1)S(1)} %copy-done.2, bf16[16,16,4,384]{3,2,1,0:T(4,128)(2,1)} %dot_general.22), kind=kOutput, calls=%fused_computation.31 | convolution fusion | flops 806354944 | bytes 3670016 | tf_op jit(solution)/shard_map/dot_general | solution.py:19
  128.8 6.7 %all-to-all-start.2 = ((bf16[16,16,4,1024]{3,1,2,0:T(8,128)(2,1)}), bf16[16,16,4,1024]{3,1,2,0:T(8,128)(2,1)S(1)}, u32[]{:S(2)}, u32[]{:S(2)}) async-start(bf16[16,16,4,1024]{3,1,2,0:T(8,128)(2,1)} %convolution_convert_fusion), calls=%async_computation.2 | async-start | bytes 4194304 | tf_op jit(solution)/shard_map/all_to_all | solution.py:139
  137.6 1.9 gather_fusion.1
  139.9 43.0 %all-to-all-done.2 = bf16[16,16,4,1024]{3,1,2,0:T(8,128)(2,1)S(1)} async-done(((bf16[16,16,4,1024]{3,1,2,0:T(8,128)(2,1)}), bf16[16,16,4,1024]{3,1,2,0:T(8,128)(2,1)S(1)}, u32[]{:S(2)}, u32[]{:S(2)}) %all-to-all-start.2) | async-done | bytes 2097184 | tf_op jit(solution)/shard_map/all_to_all | solution.py:139
  182.8 1.8 reduce
  185.9 1.8 copy.88
  187.7 5.3 %all-to-all-start.3 = ((bf16[4,32,4,1024]{3,2,0,1:T(4,128)(2,1)}), bf16[4,32,4,1024]{3,2,0,1:T(4,128)(2,1)S(1)}, u32[]{:S(2)}, u32[]{:S(2)}) async-start(bf16[4,32,4,1024]{3,2,0,1:T(4,128)(2,1)} %copy.88), calls=%async_computation.3 | async-start | bytes 2097152 | tf_op jit(solution)/shard_map/all_to_all | solution.py:146
  193.1 14.3 %all-gather.5.cloned.1.call-done = bf16[1,4096,2,128]{3,1,2,0:T(8,128)(2,1)} async-done(((bf16[1,128,2,128]{3,1,2,0:T(8,128)(2,1)}), bf16[1,4096,2,128]{3,1,2,0:T(8,128)(2,1)}) %all-gather.5.cloned.1.call-update) | async-done | bytes 2097168 | tf_op jit(solution)/shard_map/all_gather | solution.py:38
  207.4 89.6 %while.15 = (s32[]{:T(128)}, f32[2,8,128]{2,1,0:T(8,128)S(1)}, f32[2,8,128]{2,1,0:T(8,128)S(1)}, f32[2,8,128,128]{3,2,1,0:T(8,128)S(1)}, s32[8]{0:T(128)S(1)}, /...) while((s32[]{:T(128)}, f32[2,8,128]{2,1,0:T(8,128)S(1)}, ...), condition=%wide.region_3.4_spmd.clone, body=%wide.region_0.3_spmd.clone.sunk | while | flops 551365248 | bytes 32904396 | solution.py:67
  208.8 3.7 %fusion.58 = (f32[2,8,128]{2,1,0:T(8,128)S(1)}, f32[2,512,128,8]{2,1,3,0:T(8,128)}) fusion(pred[128,512]{0,1:T(8,128)(4,1)S(1)} %broadcast_compare_fusion.2, bf16[128,2,8,128]{3,0,2,1:T(8,128)(2,1)S(1)} %get-tuple-element.236, bf16[8,512,2,128]{3,1,0,2:T(8,128)(2,1)} %get-tuple-element.235, s32[]{:T(128)S(6)} %copy.107), kind=kOutput, calls=%fused_computation.6.clone.1 | convolution fusion | flops 271579136 | bytes 5054468 | tf_op jit(solution)/shard_map/while/body/eval_jaxpr/qhgd,khd->hgqk/dot_general | solution.py:49
  212.5 3.3 %fusion.59 = f32[2,8,128]{2,1,0:T(8,128)S(1)} fusion(f32[2,512,128,8]{2,1,3,0:T(8,128)} %get-tuple-element.203, f32[2,8,128]{2,1,0:T(8,128)S(1)} %select_maximum_fusion.2, pred[128,512]{0,1:T(8,128)(4,1)S(1)} %broadcast_compare_fusion.2), kind=kLoop, calls=%fused_computation.8.clone.1 | loop fusion | flops 5240832 | bytes 4276224 | tf_op jit(solution)/shard_map/while/body/eval_jaxpr/reduce_sum | solution.py:58
  216.0 2.6 fusion.61
  220.0 3.7 %fusion.58 = (f32[2,8,128]{2,1,0:T(8,128)S(1)}, f32[2,512,128,8]{2,1,3,0:T(8,128)}) fusion(pred[128,512]{0,1:T(8,128)(4,1)S(1)} %broadcast_compare_fusion.2, bf16[128,2,8,128]{3,0,2,1:T(8,128)(2,1)S(1)} %get-tuple-element.236, bf16[8,512,2,128]{3,1,0,2:T(8,128)(2,1)} %get-tuple-element.235, s32[]{:T(128)S(6)} %copy.107), kind=kOutput, calls=%fused_computation.6.clone.1 | convolution fusion | flops 271579136 | bytes 5054468 | tf_op jit(solution)/shard_map/while/body/eval_jaxpr/qhgd,khd->hgqk/dot_general | solution.py:49
  223.7 3.3 %fusion.59 = f32[2,8,128]{2,1,0:T(8,128)S(1)} fusion(f32[2,512,128,8]{2,1,3,0:T(8,128)} %get-tuple-element.203, f32[2,8,128]{2,1,0:T(8,128)S(1)} %select_maximum_fusion.2, pred[128,512]{0,1:T(8,128)(4,1)S(1)} %broadcast_compare_fusion.2), kind=kLoop, calls=%fused_computation.8.clone.1 | loop fusion | flops 5240832 | bytes 4276224 | tf_op jit(solution)/shard_map/while/body/eval_jaxpr/reduce_sum | solution.py:58
  227.2 2.6 fusion.61
  231.2 3.7 %fusion.58 = (f32[2,8,128]{2,1,0:T(8,128)S(1)}, f32[2,512,128,8]{2,1,3,0:T(8,128)}) fusion(pred[128,512]{0,1:T(8,128)(4,1)S(1)} %broadcast_compare_fusion.2, bf16[128,2,8,128]{3,0,2,1:T(8,128)(2,1)S(1)} %get-tuple-element.236, bf16[8,512,2,128]{3,1,0,2:T(8,128)(2,1)} %get-tuple-element.235, s32[]{:T(128)S(6)} %copy.107), kind=kOutput, calls=%fused_computation.6.clone.1 | convolution fusion | flops 271579136 | bytes 5054468 | tf_op jit(solution)/shard_map/while/body/eval_jaxpr/qhgd,khd->hgqk/dot_general | solution.py:49
  234.9 3.3 %fusion.59 = f32[2,8,128]{2,1,0:T(8,128)S(1)} fusion(f32[2,512,128,8]{2,1,3,0:T(8,128)} %get-tuple-element.203, f32[2,8,128]{2,1,0:T(8,128)S(1)} %select_maximum_fusion.2, pred[128,512]{0,1:T(8,128)(4,1)S(1)} %broadcast_compare_fusion.2), kind=kLoop, calls=%fused_computation.8.clone.1 | loop fusion | flops 5240832 | bytes 4276224 | tf_op jit(solution)/shard_map/while/body/eval_jaxpr/reduce_sum | solution.py:58
  238.4 2.6 fusion.61
  242.5 3.7 %fusion.58 = (f32[2,8,128]{2,1,0:T(8,128)S(1)}, f32[2,512,128,8]{2,1,3,0:T(8,128)}) fusion(pred[128,512]{0,1:T(8,128)(4,1)S(1)} %broadcast_compare_fusion.2, bf16[128,2,8,128]{3,0,2,1:T(8,128)(2,1)S(1)} %get-tuple-element.236, bf16[8,512,2,128]{3,1,0,2:T(8,128)(2,1)} %get-tuple-element.235, s32[]{:T(128)S(6)} %copy.107), kind=kOutput, calls=%fused_computation.6.clone.1 | convolution fusion | flops 271579136 | bytes 5054468 | tf_op jit(solution)/shard_map/while/body/eval_jaxpr/qhgd,khd->hgqk/dot_general | solution.py:49
  246.1 3.3 %fusion.59 = f32[2,8,128]{2,1,0:T(8,128)S(1)} fusion(f32[2,512,128,8]{2,1,3,0:T(8,128)} %get-tuple-element.203, f32[2,8,128]{2,1,0:T(8,128)S(1)} %select_maximum_fusion.2, pred[128,512]{0,1:T(8,128)(4,1)S(1)} %broadcast_compare_fusion.2), kind=kLoop, calls=%fused_computation.8.clone.1 | loop fusion | flops 5240832 | bytes 4276224 | tf_op jit(solution)/shard_map/while/body/eval_jaxpr/reduce_sum | solution.py:58
  249.6 2.6 fusion.61
  253.7 3.7 %fusion.58 = (f32[2,8,128]{2,1,0:T(8,128)S(1)}, f32[2,512,128,8]{2,1,3,0:T(8,128)}) fusion(pred[128,512]{0,1:T(8,128)(4,1)S(1)} %broadcast_compare_fusion.2, bf16[128,2,8,128]{3,0,2,1:T(8,128)(2,1)S(1)} %get-tuple-element.236, bf16[8,512,2,128]{3,1,0,2:T(8,128)(2,1)} %get-tuple-element.235, s32[]{:T(128)S(6)} %copy.107), kind=kOutput, calls=%fused_computation.6.clone.1 | convolution fusion | flops 271579136 | bytes 5054468 | tf_op jit(solution)/shard_map/while/body/eval_jaxpr/qhgd,khd->hgqk/dot_general | solution.py:49
  257.3 3.3 %fusion.59 = f32[2,8,128]{2,1,0:T(8,128)S(1)} fusion(f32[2,512,128,8]{2,1,3,0:T(8,128)} %get-tuple-element.203, f32[2,8,128]{2,1,0:T(8,128)S(1)} %select_maximum_fusion.2, pred[128,512]{0,1:T(8,128)(4,1)S(1)} %broadcast_compare_fusion.2), kind=kLoop, calls=%fused_computation.8.clone.1 | loop fusion | flops 5240832 | bytes 4276224 | tf_op jit(solution)/shard_map/while/body/eval_jaxpr/reduce_sum | solution.py:58
  260.8 2.6 fusion.61
  264.9 3.7 %fusion.58 = (f32[2,8,128]{2,1,0:T(8,128)S(1)}, f32[2,512,128,8]{2,1,3,0:T(8,128)}) fusion(pred[128,512]{0,1:T(8,128)(4,1)S(1)} %broadcast_compare_fusion.2, bf16[128,2,8,128]{3,0,2,1:T(8,128)(2,1)S(1)} %get-tuple-element.236, bf16[8,512,2,128]{3,1,0,2:T(8,128)(2,1)} %get-tuple-element.235, s32[]{:T(128)S(6)} %copy.107), kind=kOutput, calls=%fused_computation.6.clone.1 | convolution fusion | flops 271579136 | bytes 5054468 | tf_op jit(solution)/shard_map/while/body/eval_jaxpr/qhgd,khd->hgqk/dot_general | solution.py:49
  268.6 3.3 %fusion.59 = f32[2,8,128]{2,1,0:T(8,128)S(1)} fusion(f32[2,512,128,8]{2,1,3,0:T(8,128)} %get-tuple-element.203, f32[2,8,128]{2,1,0:T(8,128)S(1)} %select_maximum_fusion.2, pred[128,512]{0,1:T(8,128)(4,1)S(1)} %broadcast_compare_fusion.2), kind=kLoop, calls=%fused_computation.8.clone.1 | loop fusion | flops 5240832 | bytes 4276224 | tf_op jit(solution)/shard_map/while/body/eval_jaxpr/reduce_sum | solution.py:58
  272.0 2.6 fusion.61
  276.1 3.7 %fusion.58 = (f32[2,8,128]{2,1,0:T(8,128)S(1)}, f32[2,512,128,8]{2,1,3,0:T(8,128)}) fusion(pred[128,512]{0,1:T(8,128)(4,1)S(1)} %broadcast_compare_fusion.2, bf16[128,2,8,128]{3,0,2,1:T(8,128)(2,1)S(1)} %get-tuple-element.236, bf16[8,512,2,128]{3,1,0,2:T(8,128)(2,1)} %get-tuple-element.235, s32[]{:T(128)S(6)} %copy.107), kind=kOutput, calls=%fused_computation.6.clone.1 | convolution fusion | flops 271579136 | bytes 5054468 | tf_op jit(solution)/shard_map/while/body/eval_jaxpr/qhgd,khd->hgqk/dot_general | solution.py:49
  279.8 3.3 %fusion.59 = f32[2,8,128]{2,1,0:T(8,128)S(1)} fusion(f32[2,512,128,8]{2,1,3,0:T(8,128)} %get-tuple-element.203, f32[2,8,128]{2,1,0:T(8,128)S(1)} %select_maximum_fusion.2, pred[128,512]{0,1:T(8,128)(4,1)S(1)} %broadcast_compare_fusion.2), kind=kLoop, calls=%fused_computation.8.clone.1 | loop fusion | flops 5240832 | bytes 4276224 | tf_op jit(solution)/shard_map/while/body/eval_jaxpr/reduce_sum | solution.py:58
  283.2 2.6 fusion.61
  287.3 3.7 %fusion.58 = (f32[2,8,128]{2,1,0:T(8,128)S(1)}, f32[2,512,128,8]{2,1,3,0:T(8,128)}) fusion(pred[128,512]{0,1:T(8,128)(4,1)S(1)} %broadcast_compare_fusion.2, bf16[128,2,8,128]{3,0,2,1:T(8,128)(2,1)S(1)} %get-tuple-element.236, bf16[8,512,2,128]{3,1,0,2:T(8,128)(2,1)} %get-tuple-element.235, s32[]{:T(128)S(6)} %copy.107), kind=kOutput, calls=%fused_computation.6.clone.1 | convolution fusion | flops 271579136 | bytes 5054468 | tf_op jit(solution)/shard_map/while/body/eval_jaxpr/qhgd,khd->hgqk/dot_general | solution.py:49
  291.0 3.3 %fusion.59 = f32[2,8,128]{2,1,0:T(8,128)S(1)} fusion(f32[2,512,128,8]{2,1,3,0:T(8,128)} %get-tuple-element.203, f32[2,8,128]{2,1,0:T(8,128)S(1)} %select_maximum_fusion.2, pred[128,512]{0,1:T(8,128)(4,1)S(1)} %broadcast_compare_fusion.2), kind=kLoop, calls=%fused_computation.8.clone.1 | loop fusion | flops 5240832 | bytes 4276224 | tf_op jit(solution)/shard_map/while/body/eval_jaxpr/reduce_sum | solution.py:58
  294.4 2.6 fusion.61
  300.6 2.3 multiply_reduce_fusion
  (146 shorter events, 23.0 us)
Async XLA Ops:
  7.2 130.2 %copy-start = (bf16[1024,128]{1,0:T(8,128)(2,1)S(1)}, bf16[1024,128]{1,0:T(8,128)(2,1)}, u32[]{:S(2)}) copy-start(bf16[1024,128]{1,0:T(8,128)(2,1)} %param.18) | copy-start | bytes 786436
  14.8 14.8 %copy-start.7 = (bf16[1,128,2,128]{3,2,1,0:T(2,128)(2,1)S(1)}, bf16[1,128,2,128]{3,2,1,0:T(2,128)(2,1)}, u32[]{:S(2)}) copy-start(bf16[1,128,2,128]{3,2,1,0:T(2,128)(2,1)} %param.14) | copy-start | bytes 196612
  16.4 41.3 %all-to-all-start = ((bf16[4,32,4,1024]{3,2,0,1:T(4,128)(2,1)}), bf16[4,32,4,1024]{3,2,0,1:T(4,128)(2,1)S(1)}, u32[]{:S(2)}, u32[]{:S(2)}) async-start(bf16[4,32,4,1024]{3,2,0,1:T(4,128)(2,1)} %copy.84), calls=%async_computation | async-start | bytes 2097152 | tf_op jit(solution)/shard_map/all_to_all | solution.py:121
  29.5 163.6 %all-gather.3.cloned.1.call-start = ((), (), s32[]{:S(2)}) async-start(), calls=%async_computation.4 | async-start | bytes 2162688 | tf_op jit(solution)/shard_map/all_gather | solution.py:37
  60.2 7.6 %copy-start.4 = (bf16[192,1024]{1,0:T(8,128)(2,1)S(1)}, bf16[192,1024]{1,0:T(8,128)(2,1)}, u32[]{:S(2)}) copy-start(bf16[192,1024]{1,0:T(8,128)(2,1)} %param.21) | copy-start | bytes 1179652
  60.2 7.6 %copy-start.5 = (bf16[192,1024]{1,0:T(8,128)(2,1)S(1)}, bf16[192,1024]{1,0:T(8,128)(2,1)}, u32[]{:S(2)}) copy-start(bf16[192,1024]{1,0:T(8,128)(2,1)} %param.20) | copy-start | bytes 1179652
  60.2 11.9 %copy-start.8 = (bf16[1,128,2,128]{3,2,1,0:T(2,128)(2,1)S(1)}, bf16[1,128,2,128]{3,2,1,0:T(2,128)(2,1)}, u32[]{:S(2)}) copy-start(bf16[1,128,2,128]{3,2,1,0:T(2,128)(2,1)} %param.15) | copy-start | bytes 196612
  60.2 55.0 %all-to-all-start.1 = ((bf16[16,16,4,1024]{3,2,1,0:T(4,128)(2,1)}), bf16[16,16,4,1024]{3,2,1,0:T(4,128)(2,1)S(1)}, u32[]{:S(2)}, u32[]{:S(2)}) async-start(bf16[16,16,4,1024]{3,2,1,0:T(4,128)(2,1)} %bitcast.120), calls=%async_computation.1 | async-start | bytes 4194304 | tf_op jit(solution)/shard_map/all_to_all | solution.py:137
  67.8 139.7 %all-gather.5.cloned.1.call-start = ((), (), s32[]{:S(2)}) async-start(), calls=%async_computation.5 | async-start | bytes 2162688 | tf_op jit(solution)/shard_map/all_gather | solution.py:38
  70.0 5.1 %collective-permute-start = (bf16[3,192,1024]{2,1,0:T(8,128)(2,1)}, bf16[3,192,1024]{2,1,0:T(8,128)(2,1)}, u32[]{:S(2)}, u32[]{:S(2)}) collective-permute-start(bf16[3,192,1024]{2,1,0:T(8,128)(2,1)} %pad_maximum_fusion), channel_id=1, source_target_pairs={{0,1},{1,0},{2,3},{3,2},{4,5},{5,4},{6,7},{7,6},{8,9},{9,8},{10,11... | collective-permute-start | bytes 3538952 | tf_op jit(solution)/shard_map/ppermute | solution.py:9
  117.2 3.2 %copy-start.2 = (bf16[3,384,1024]{2,1,0:T(8,128)(2,1)S(1)}, bf16[3,384,1024]{2,1,0:T(8,128)(2,1)}, u32[]{:S(2)}) copy-start(bf16[3,384,1024]{2,1,0:T(8,128)(2,1)} %maximum_select_fusion) | copy-start | bytes 7077892
  117.2 3.2 %copy-start.3 = (bf16[1024,1024]{1,0:T(8,128)(2,1)S(1)}, bf16[1024,1024]{1,0:T(8,128)(2,1)}, u32[]{:S(2)}) copy-start(bf16[1024,1024]{1,0:T(8,128)(2,1)} %reshape.284) | copy-start | bytes 6291460
  128.8 8.1 %copy-start.9 = (s32[1,128,2]{1,2,0:T(2,128)S(1)}, s32[1,128,2]{1,2,0:T(2,128)}, u32[]{:S(2)}) copy-start(s32[1,128,2]{1,2,0:T(2,128)} %param.16) | copy-start | bytes 3076
  128.8 54.1 %all-to-all-start.2 = ((bf16[16,16,4,1024]{3,1,2,0:T(8,128)(2,1)}), bf16[16,16,4,1024]{3,1,2,0:T(8,128)(2,1)S(1)}, u32[]{:S(2)}, u32[]{:S(2)}) async-start(bf16[16,16,4,1024]{3,1,2,0:T(8,128)(2,1)} %convolution_convert_fusion), calls=%async_computation.2 | async-start | bytes 4194304 | tf_op jit(solution)/shard_map/all_to_all | solution.py:139
  185.9 21.5 %copy-start.6 = (f32[2,8,128,128]{3,2,1,0:T(8,128)S(1)}, f32[2,8,128,128]{3,2,1,0:T(8,128)}, u32[]{:S(2)}) copy-start(f32[2,8,128,128]{3,2,1,0:T(8,128)} %custom-call.4) | copy-start | bytes 3145732
  187.7 110.8 %all-to-all-start.3 = ((bf16[4,32,4,1024]{3,2,0,1:T(4,128)(2,1)}), bf16[4,32,4,1024]{3,2,0,1:T(4,128)(2,1)S(1)}, u32[]{:S(2)}, u32[]{:S(2)}) async-start(bf16[4,32,4,1024]{3,2,0,1:T(4,128)(2,1)} %copy.88), calls=%async_computation.3 | async-start | bytes 2097152 | tf_op jit(solution)/shard_map/all_to_all | solution.py:146
  212.5 3.4 %copy-start.1 = (f32[2,512,128,8]{2,1,3,0:T(8,128)S(1)}, f32[2,512,128,8]{2,1,3,0:T(8,128)}, u32[]{:S(2)}) copy-start(f32[2,512,128,8]{2,1,3,0:T(8,128)} %get-tuple-element.203) | copy-start | bytes 12582916 | tf_op jit(solution)/shard_map/while
  223.7 3.4 %copy-start.1 = (f32[2,512,128,8]{2,1,3,0:T(8,128)S(1)}, f32[2,512,128,8]{2,1,3,0:T(8,128)}, u32[]{:S(2)}) copy-start(f32[2,512,128,8]{2,1,3,0:T(8,128)} %get-tuple-element.203) | copy-start | bytes 12582916 | tf_op jit(solution)/shard_map/while
  234.9 3.4 %copy-start.1 = (f32[2,512,128,8]{2,1,3,0:T(8,128)S(1)}, f32[2,512,128,8]{2,1,3,0:T(8,128)}, u32[]{:S(2)}) copy-start(f32[2,512,128,8]{2,1,3,0:T(8,128)} %get-tuple-element.203) | copy-start | bytes 12582916 | tf_op jit(solution)/shard_map/while
  246.1 3.4 %copy-start.1 = (f32[2,512,128,8]{2,1,3,0:T(8,128)S(1)}, f32[2,512,128,8]{2,1,3,0:T(8,128)}, u32[]{:S(2)}) copy-start(f32[2,512,128,8]{2,1,3,0:T(8,128)} %get-tuple-element.203) | copy-start | bytes 12582916 | tf_op jit(solution)/shard_map/while
  257.3 3.4 %copy-start.1 = (f32[2,512,128,8]{2,1,3,0:T(8,128)S(1)}, f32[2,512,128,8]{2,1,3,0:T(8,128)}, u32[]{:S(2)}) copy-start(f32[2,512,128,8]{2,1,3,0:T(8,128)} %get-tuple-element.203) | copy-start | bytes 12582916 | tf_op jit(solution)/shard_map/while
  268.5 3.4 %copy-start.1 = (f32[2,512,128,8]{2,1,3,0:T(8,128)S(1)}, f32[2,512,128,8]{2,1,3,0:T(8,128)}, u32[]{:S(2)}) copy-start(f32[2,512,128,8]{2,1,3,0:T(8,128)} %get-tuple-element.203) | copy-start | bytes 12582916 | tf_op jit(solution)/shard_map/while
  279.7 3.4 %copy-start.1 = (f32[2,512,128,8]{2,1,3,0:T(8,128)S(1)}, f32[2,512,128,8]{2,1,3,0:T(8,128)}, u32[]{:S(2)}) copy-start(f32[2,512,128,8]{2,1,3,0:T(8,128)} %get-tuple-element.203) | copy-start | bytes 12582916 | tf_op jit(solution)/shard_map/while
  290.9 3.4 %copy-start.1 = (f32[2,512,128,8]{2,1,3,0:T(8,128)S(1)}, f32[2,512,128,8]{2,1,3,0:T(8,128)}, u32[]{:S(2)}) copy-start(f32[2,512,128,8]{2,1,3,0:T(8,128)} %get-tuple-element.203) | copy-start | bytes 12582916 | tf_op jit(solution)/shard_map/while
Sparse Core Ops, SparseCore 0:
  34.1 84.8 all-gather.2
  122.8 84.6 all-gather.4
where the time goes:
time: 311 us; the launch traced here: 310 us
  waiting for transfers between devices  124 us (40%)
  matrix products  60 us (19%)
  other arithmetic  41.4 us (13%)
  starting transfers between devices  34.9 us (11%)
  local copies, waits for them, and re-layouts  29.7 us (10%)
  between operations  14.4 us (5%)
  loops' own time  5.69 us (2%)
    all_to_all x1, waiting for transfers between devices, local(): lax.all_to_all(partials.astype(jnp.bfloat16), 'exp', split_axis=0, concat...  43 us
    all_to_all x1, waiting for transfers between devices, local(): lax.all_to_all(spread_rows, 'exp', split_axis=0, concat_axis=0, tiled=True)  36.6 us
    dot_general x8, matrix products, advance(): jnp.einsum('qhgd,khd->hgqk', grouped, key_block, preferred_element_type=j...  29.5 us
    all_to_all x1, waiting for transfers between devices, local(): lax.all_to_all(outgoing, 'ctx', split_axis=1, concat_axis=1, tiled=True)  27.4 us
    reduce_sum x8, other arithmetic, advance(): totals = totals * factor + jnp.sum(weights, axis=-1)  26.6 us
    dot_general x8, matrix products, advance(): jnp.einsum('hgqk,khd->hgqd', weights.astype(jnp.bfloat16), value_block, p...  21.1 us
    all_gather x1, waiting for transfers between devices, attention(): value_piece = lax.all_gather(value_rows, 'ctx', axis=1, tiled=True)  14.3 us
    all_to_all x1, starting transfers between devices, local(): lax.all_to_all(outgoing, 'ctx', split_axis=1, concat_axis=1, tiled=True)  13.2 us
  transfers between devices with their start and end apart: 7, of which 5 were waited for; matrix products, arithmetic and copies ran while one was open for 38% of the time, Pallas kernels for 0%

commit v1 on v0

--- a/solution.py
+++ b/solution.py
@@ -3,6 +3,22 @@
 import jax.numpy as jnp
 from jax import lax
 from jax.sharding import PartitionSpec as P
+
+
+def swapped_with_each(x, axis, split, join):
+    ways, here = (lax.axis_size(axis), lax.axis_index(axis))
+    width = x.shape[split] // ways
+    dims = list(x.shape)
+    dims[split] = width
+    height = dims[join]
+    dims[join] = height * ways
+    full = jnp.zeros(dims, x.dtype)
+    for mask in range(ways):
+        part = lax.dynamic_slice_in_dim(x, (here ^ mask) * width, width, axis=split)
+        if mask:
+            part = lax.ppermute(part, axis, [(d, d ^ mask) for d in range(ways)])
+        full = lax.dynamic_update_slice_in_dim(full, part, (here ^ mask) * height, axis=join)
+    return full
 
 
 def from_partner(value, axis, bit):
@@ -134,7 +150,7 @@
         halves_rows, (per_ctx, quarters // 2, 2, half_ctx, capacity, features)
     )
     spread_rows = spread_rows.reshape(exp_count, half_ctx, capacity, features)
-    received = lax.all_to_all(spread_rows, "exp", split_axis=0, concat_axis=0, tiled=True)
+    received = swapped_with_each(spread_rows, "exp", 0, 0)
     partials = expert_rows(received, held[0], held[1], held[2])
     returned = lax.all_to_all(
         partials.astype(jnp.bfloat16), "exp", split_axis=0, concat_axis=0, tiled=True

time: 311 us -> 337 us (1.084)
  the two profiles are of different devices: /device:TPU:16 before, /device:TPU:1 now
where the time goes in v1:
time: 337 us; the launch traced here: 335 us
  starting transfers between devices  102 us (30%)
  waiting for transfers between devices  80.4 us (24%)
  matrix products  60.2 us (18%)
  other arithmetic  40.3 us (12%)
  local copies, waits for them, and re-layouts  32.5 us (10%)
  between operations  14.8 us (4%)
  loops' own time  5.71 us (2%)
    ppermute x15, starting transfers between devices, swapped_with_each(): part = lax.ppermute(part, axis, [(d, d ^ mask) for d in range(ways)])  71.1 us
    all_to_all x1, waiting for transfers between devices, local(): lax.all_to_all(partials.astype(jnp.bfloat16), 'exp', split_axis=0, concat...  44.6 us
    dot_general x8, matrix products, advance(): jnp.einsum('qhgd,khd->hgqk', grouped, key_block, preferred_element_type=j...  29.6 us
    reduce_sum x8, other arithmetic, advance(): totals = totals * factor + jnp.sum(weights, axis=-1)  26.6 us
    all_to_all x1, waiting for transfers between devices, local(): lax.all_to_all(outgoing, 'ctx', split_axis=1, concat_axis=1, tiled=True)  23.2 us
    dot_general x8, matrix products, advance(): jnp.einsum('hgqk,khd->hgqd', weights.astype(jnp.bfloat16), value_block, p...  21.1 us
    all_to_all x1, starting transfers between devices, local(): lax.all_to_all(outgoing, 'ctx', split_axis=1, concat_axis=1, tiled=True)  13.8 us
    ppermute x15, waiting for transfers between devices, swapped_with_each(): part = lax.ppermute(part, axis, [(d, d ^ mask) for d in range(ways)])  12.6 us
  transfers between devices with their start and end apart: 21, of which 5 were waited for; matrix products, arithmetic and copies ran while one was open for 38% of the time, Pallas kernels for 0%

profile of v1, /device:TPU:1, one launch (start us, length us, event | category | flops | bytes accessed | tf_op | source)
XLA Modules:
  0.0 335.5 jit_solution(6848522568322075552)
XLA Ops:
  17.9 13.8 %all-to-all-start = ((bf16[4,32,4,1024]{3,2,0,1:T(4,128)(2,1)}), bf16[4,32,4,1024]{3,2,0,1:T(4,128)(2,1)S(1)}, u32[]{:S(2)}, u32[]{:S(2)}) async-start(bf16[4,32,4,1024]{3,2,0,1:T(4,128)(2,1)} %copy.84), calls=%async_computation | async-start | bytes 2097152 | tf_op jit(solution)/shard_map/all_to_all | solution.py:137
  33.0 2.9 collective-permute-start.15
  36.6 23.2 %all-to-all-done = bf16[4,32,4,1024]{3,2,0,1:T(4,128)(2,1)S(1)} async-done(((bf16[4,32,4,1024]{3,2,0,1:T(4,128)(2,1)}), bf16[4,32,4,1024]{3,2,0,1:T(4,128)(2,1)S(1)}, u32[]{:S(2)}, u32[]{:S(2)}) %all-to-all-start) | async-done | bytes 1048608 | tf_op jit(solution)/shard_map/all_to_all | solution.py:137
  63.2 5.1 %collective-permute-start = (bf16[1,16,4,1024]{3,2,1,0:T(4,128)(2,1)S(1)}, bf16[1,16,4,1024]{3,2,1,0:T(4,128)(2,1)S(1)}, u32[]{:S(2)}, u32[]{:S(2)}) collective-permute-start(bf16[1,16,4,1024]{3,2,1,0:T(4,128)(2,1)S(1)} %get-tuple-element.157), channel_id=1, source_target_pairs={{0,1},{1,0},{2,3},{3,2},{4,5},{5,4},{6,7},{7,6},{8,9},{9,8},{10,11... | collective-permute-start | bytes 393224 | tf_op jit(solution)/shard_map/ppermute | solution.py:19
  68.3 3.2 collective-permute-start.1
  71.5 3.4 %maximum_select_fusion = bf16[3,384,1024]{2,1,0:T(8,128)(2,1)} fusion(bf16[1,192,1024]{2,1,0:T(8,128)(2,1)S(1)} %bitcast.126, bf16[1,192,1024]{2,1,0:T(8,128)(2,1)S(1)} %bitcast.128, bf16[1,192,1024]{2,1,0:T(8,128)(2,1)S(1)} %bitcast.130, bf16[3,192,1024]{2,1,0:T(8,128)(2,1)} %collective-permute-done.15, pred[]{:T(512)S(6)} %eq.35), kind=kLoop, calls=%fused_computation.30 | loop fusion | flops 20054016 | bytes 4718593 | tf_op jit(solution)/shard_map/jit(_where)/select_n | solution.py:142
  77.1 4.2 %collective-permute-start.3 = (bf16[1,16,4,1024]{3,2,1,0:T(4,128)(2,1)S(1)}, bf16[1,16,4,1024]{3,2,1,0:T(4,128)(2,1)S(1)}, u32[]{:S(2)}, u32[]{:S(2)}) collective-permute-start(bf16[1,16,4,1024]{3,2,1,0:T(4,128)(2,1)S(1)} %get-tuple-element.154), channel_id=1, source_target_pairs={{0,4},{1,5},{2,6},{3,7},{4,0},{5,1},{6,2},{7,3},{8,12},{9,13},{10,... | collective-permute-start | bytes 393224 | tf_op jit(solution)/shard_map/ppermute | solution.py:19
  83.7 5.3 %collective-permute-start.5 = (bf16[1,16,4,1024]{3,2,1,0:T(4,128)(2,1)S(1)}, bf16[1,16,4,1024]{3,2,1,0:T(4,128)(2,1)S(1)}, u32[]{:S(2)}, u32[]{:S(2)}) collective-permute-start(bf16[1,16,4,1024]{3,2,1,0:T(4,128)(2,1)S(1)} %get-tuple-element.152), channel_id=1, source_target_pairs={{0,6},{1,7},{2,4},{3,5},{4,2},{5,3},{6,0},{7,1},{8,14},{9,15},{10,... | collective-permute-start | bytes 393224 | tf_op jit(solution)/shard_map/ppermute | solution.py:19
  91.2 7.4 %collective-permute-start.7 = (bf16[1,16,4,1024]{3,2,1,0:T(4,128)(2,1)S(1)}, bf16[1,16,4,1024]{3,2,1,0:T(4,128)(2,1)S(1)}, u32[]{:S(2)}, u32[]{:S(2)}) collective-permute-start(bf16[1,16,4,1024]{3,2,1,0:T(4,128)(2,1)S(1)} %get-tuple-element.150), channel_id=1, source_target_pairs={{0,8},{1,9},{2,10},{3,11},{4,12},{5,13},{6,14},{7,15},{8,0},{9,1},... | collective-permute-start | bytes 393224 | tf_op jit(solution)/shard_map/ppermute | solution.py:19
  98.7 6.1 %collective-permute-start.8 = (bf16[1,16,4,1024]{3,2,1,0:T(4,128)(2,1)S(1)}, bf16[1,16,4,1024]{3,2,1,0:T(4,128)(2,1)S(1)}, u32[]{:S(2)}, u32[]{:S(2)}) collective-permute-start(bf16[1,16,4,1024]{3,2,1,0:T(4,128)(2,1)S(1)} %get-tuple-element.149), channel_id=1, source_target_pairs={{0,9},{1,8},{2,11},{3,10},{4,13},{5,12},{6,15},{7,14},{8,1},{9,0},... | collective-permute-start | bytes 393224 | tf_op jit(solution)/shard_map/ppermute | solution.py:19
  106.9 16.7 %collective-permute-start.10 = (bf16[1,16,4,1024]{3,2,1,0:T(4,128)(2,1)S(1)}, bf16[1,16,4,1024]{3,2,1,0:T(4,128)(2,1)S(1)}, u32[]{:S(2)}, u32[]{:S(2)}) collective-permute-start(bf16[1,16,4,1024]{3,2,1,0:T(4,128)(2,1)S(1)} %get-tuple-element.147), channel_id=1, source_target_pairs={{0,11},{1,10},{2,9},{3,8},{4,15},{5,14},{6,13},{7,12},{8,3},{9,2},... | collective-permute-start | bytes 393224 | tf_op jit(solution)/shard_map/ppermute | solution.py:19
  123.6 3.9 %collective-permute-start.11 = (bf16[1,16,4,1024]{3,2,1,0:T(4,128)(2,1)S(1)}, bf16[1,16,4,1024]{3,2,1,0:T(4,128)(2,1)S(1)}, u32[]{:S(2)}, u32[]{:S(2)}) collective-permute-start(bf16[1,16,4,1024]{3,2,1,0:T(4,128)(2,1)S(1)} %get-tuple-element.146), channel_id=1, source_target_pairs={{0,12},{1,13},{2,14},{3,15},{4,8},{5,9},{6,10},{7,11},{8,4},{9,5},... | collective-permute-start | bytes 393224 | tf_op jit(solution)/shard_map/ppermute | solution.py:19
  127.6 3.2 collective-permute-start.12
  132.9 5.6 %collective-permute-start.14 = (bf16[1,16,4,1024]{3,2,1,0:T(4,128)(2,1)S(1)}, bf16[1,16,4,1024]{3,2,1,0:T(4,128)(2,1)S(1)}, u32[]{:S(2)}, u32[]{:S(2)}) collective-permute-start(bf16[1,16,4,1024]{3,2,1,0:T(4,128)(2,1)S(1)} %get-tuple-element.143), channel_id=1, source_target_pairs={{0,15},{1,14},{2,13},{3,12},{4,11},{5,10},{6,9},{7,8},{8,7},{9,6},... | collective-permute-start | bytes 393224 | tf_op jit(solution)/shard_map/ppermute | solution.py:19
  138.7 5.6 %collective-permute-done.12 = bf16[1,16,4,1024]{3,2,1,0:T(4,128)(2,1)S(1)} collective-permute-done((bf16[1,16,4,1024]{3,2,1,0:T(4,128)(2,1)S(1)}, bf16[1,16,4,1024]{3,2,1,0:T(4,128)(2,1)S(1)}, u32[]{:S(2)}, u32[]{:S(2)}) %collective-permute-start.12) | collective-permute-done | bytes 131104 | tf_op jit(solution)/shard_map/ppermute | solution.py:19
  144.4 3.7 %collective-permute-done.13 = bf16[1,16,4,1024]{3,2,1,0:T(4,128)(2,1)S(1)} collective-permute-done((bf16[1,16,4,1024]{3,2,1,0:T(4,128)(2,1)S(1)}, bf16[1,16,4,1024]{3,2,1,0:T(4,128)(2,1)S(1)}, u32[]{:S(2)}, u32[]{:S(2)}) %collective-permute-start.13) | collective-permute-done | bytes 131104 | tf_op jit(solution)/shard_map/ppermute | solution.py:19
  148.1 3.3 collective-permute-done.14
  153.6 3.2 fusion.23
  159.1 2.4 dot_general.22
  161.5 3.7 %convolution_convert_fusion = bf16[16,16,4,1024]{3,1,2,0:T(8,128)(2,1)} fusion(bf16[3,384,1024]{2,1,0:T(8,128)(2,1)S(1)} %copy-done.2, bf16[16,16,4,384]{3,2,1,0:T(4,128)(2,1)} %dot_general.22), kind=kOutput, calls=%fused_computation.31 | convolution fusion | flops 806354944 | bytes 3670016 | tf_op jit(solution)/shard_map/dot_general | solution.py:35
  165.3 8.6 %all-to-all-start.1 = ((bf16[16,16,4,1024]{3,1,2,0:T(8,128)(2,1)}), bf16[16,16,4,1024]{3,1,2,0:T(8,128)(2,1)S(1)}, u32[]{:S(2)}, u32[]{:S(2)}) async-start(bf16[16,16,4,1024]{3,1,2,0:T(8,128)(2,1)} %convolution_convert_fusion), calls=%async_computation.1 | async-start | bytes 4194304 | tf_op jit(solution)/shard_map/all_to_all | solution.py:155
  178.2 44.6 %all-to-all-done.1 = bf16[16,16,4,1024]{3,1,2,0:T(8,128)(2,1)S(1)} async-done(((bf16[16,16,4,1024]{3,1,2,0:T(8,128)(2,1)}), bf16[16,16,4,1024]{3,1,2,0:T(8,128)(2,1)S(1)}, u32[]{:S(2)}, u32[]{:S(2)}) %all-to-all-start.1) | async-done | bytes 2097184 | tf_op jit(solution)/shard_map/all_to_all | solution.py:155
  227.7 5.1 %all-to-all-start.2 = ((bf16[4,32,4,1024]{3,2,0,1:T(4,128)(2,1)}), bf16[4,32,4,1024]{3,2,0,1:T(4,128)(2,1)S(1)}, u32[]{:S(2)}, u32[]{:S(2)}) async-start(bf16[4,32,4,1024]{3,2,0,1:T(4,128)(2,1)} %copy.88), calls=%async_computation.2 | async-start | bytes 2097152 | tf_op jit(solution)/shard_map/all_to_all | solution.py:162
  232.9 89.9 %while.15 = (s32[]{:T(128)}, f32[2,8,128]{2,1,0:T(8,128)S(1)}, f32[2,8,128]{2,1,0:T(8,128)S(1)}, f32[2,8,128,128]{3,2,1,0:T(8,128)S(1)}, s32[8]{0:T(128)S(1)}, /...) while((s32[]{:T(128)}, f32[2,8,128]{2,1,0:T(8,128)S(1)}, ...), condition=%wide.region_3.4_spmd.clone, body=%wide.region_0.3_spmd.clone.sunk | while | flops 551365248 | bytes 32905404 | solution.py:83
  234.3 3.7 %fusion.59 = (f32[2,8,128]{2,1,0:T(8,128)S(1)}, f32[2,512,128,8]{2,1,3,0:T(8,128)}) fusion(pred[128,512]{0,1:T(8,128)(4,1)S(1)} %broadcast_compare_fusion.2, bf16[128,2,8,128]{3,0,2,1:T(8,128)(2,1)S(1)} %get-tuple-element.252, bf16[8,512,2,128]{3,1,0,2:T(8,128)(2,1)} %get-tuple-element.251, s32[]{:T(128)} %get-tuple-element.234), kind=kOutput, calls=%fused_computation.6.clone.1 | convolution fusion | flops 271579136 | bytes 5054976 | tf_op jit(solution)/shard_map/while/body/eval_jaxpr/qhgd,khd->hgqk/dot_general | solution.py:65
  238.0 3.3 fusion.60
  241.4 2.6 fusion.62
  245.5 3.7 %fusion.59 = (f32[2,8,128]{2,1,0:T(8,128)S(1)}, f32[2,512,128,8]{2,1,3,0:T(8,128)}) fusion(pred[128,512]{0,1:T(8,128)(4,1)S(1)} %broadcast_compare_fusion.2, bf16[128,2,8,128]{3,0,2,1:T(8,128)(2,1)S(1)} %get-tuple-element.252, bf16[8,512,2,128]{3,1,0,2:T(8,128)(2,1)} %get-tuple-element.251, s32[]{:T(128)} %get-tuple-element.234), kind=kOutput, calls=%fused_computation.6.clone.1 | convolution fusion | flops 271579136 | bytes 5054976 | tf_op jit(solution)/shard_map/while/body/eval_jaxpr/qhgd,khd->hgqk/dot_general | solution.py:65
  249.2 3.3 fusion.60
  252.7 2.6 fusion.62
  256.7 3.7 %fusion.59 = (f32[2,8,128]{2,1,0:T(8,128)S(1)}, f32[2,512,128,8]{2,1,3,0:T(8,128)}) fusion(pred[128,512]{0,1:T(8,128)(4,1)S(1)} %broadcast_compare_fusion.2, bf16[128,2,8,128]{3,0,2,1:T(8,128)(2,1)S(1)} %get-tuple-element.252, bf16[8,512,2,128]{3,1,0,2:T(8,128)(2,1)} %get-tuple-element.251, s32[]{:T(128)} %get-tuple-element.234), kind=kOutput, calls=%fused_computation.6.clone.1 | convolution fusion | flops 271579136 | bytes 5054976 | tf_op jit(solution)/shard_map/while/body/eval_jaxpr/qhgd,khd->hgqk/dot_general | solution.py:65
  260.5 3.3 fusion.60
  263.9 2.6 fusion.62
  268.0 3.7 %fusion.59 = (f32[2,8,128]{2,1,0:T(8,128)S(1)}, f32[2,512,128,8]{2,1,3,0:T(8,128)}) fusion(pred[128,512]{0,1:T(8,128)(4,1)S(1)} %broadcast_compare_fusion.2, bf16[128,2,8,128]{3,0,2,1:T(8,128)(2,1)S(1)} %get-tuple-element.252, bf16[8,512,2,128]{3,1,0,2:T(8,128)(2,1)} %get-tuple-element.251, s32[]{:T(128)} %get-tuple-element.234), kind=kOutput, calls=%fused_computation.6.clone.1 | convolution fusion | flops 271579136 | bytes 5054976 | tf_op jit(solution)/shard_map/while/body/eval_jaxpr/qhgd,khd->hgqk/dot_general | solution.py:65
  271.7 3.3 fusion.60
  275.1 2.6 fusion.62
  279.2 3.7 %fusion.59 = (f32[2,8,128]{2,1,0:T(8,128)S(1)}, f32[2,512,128,8]{2,1,3,0:T(8,128)}) fusion(pred[128,512]{0,1:T(8,128)(4,1)S(1)} %broadcast_compare_fusion.2, bf16[128,2,8,128]{3,0,2,1:T(8,128)(2,1)S(1)} %get-tuple-element.252, bf16[8,512,2,128]{3,1,0,2:T(8,128)(2,1)} %get-tuple-element.251, s32[]{:T(128)} %get-tuple-element.234), kind=kOutput, calls=%fused_computation.6.clone.1 | convolution fusion | flops 271579136 | bytes 5054976 | tf_op jit(solution)/shard_map/while/body/eval_jaxpr/qhgd,khd->hgqk/dot_general | solution.py:65
  282.9 3.3 fusion.60
  286.4 2.6 fusion.62
  290.4 3.7 %fusion.59 = (f32[2,8,128]{2,1,0:T(8,128)S(1)}, f32[2,512,128,8]{2,1,3,0:T(8,128)}) fusion(pred[128,512]{0,1:T(8,128)(4,1)S(1)} %broadcast_compare_fusion.2, bf16[128,2,8,128]{3,0,2,1:T(8,128)(2,1)S(1)} %get-tuple-element.252, bf16[8,512,2,128]{3,1,0,2:T(8,128)(2,1)} %get-tuple-element.251, s32[]{:T(128)} %get-tuple-element.234), kind=kOutput, calls=%fused_computation.6.clone.1 | convolution fusion | flops 271579136 | bytes 5054976 | tf_op jit(solution)/shard_map/while/body/eval_jaxpr/qhgd,khd->hgqk/dot_general | solution.py:65
  294.2 3.3 fusion.60
  297.6 2.6 fusion.62
  301.7 3.7 %fusion.59 = (f32[2,8,128]{2,1,0:T(8,128)S(1)}, f32[2,512,128,8]{2,1,3,0:T(8,128)}) fusion(pred[128,512]{0,1:T(8,128)(4,1)S(1)} %broadcast_compare_fusion.2, bf16[128,2,8,128]{3,0,2,1:T(8,128)(2,1)S(1)} %get-tuple-element.252, bf16[8,512,2,128]{3,1,0,2:T(8,128)(2,1)} %get-tuple-element.251, s32[]{:T(128)} %get-tuple-element.234), kind=kOutput, calls=%fused_computation.6.clone.1 | convolution fusion | flops 271579136 | bytes 5054976 | tf_op jit(solution)/shard_map/while/body/eval_jaxpr/qhgd,khd->hgqk/dot_general | solution.py:65
  305.4 3.3 fusion.60
  308.8 2.6 fusion.62
  312.9 3.7 %fusion.59 = (f32[2,8,128]{2,1,0:T(8,128)S(1)}, f32[2,512,128,8]{2,1,3,0:T(8,128)}) fusion(pred[128,512]{0,1:T(8,128)(4,1)S(1)} %broadcast_compare_fusion.2, bf16[128,2,8,128]{3,0,2,1:T(8,128)(2,1)S(1)} %get-tuple-element.252, bf16[8,512,2,128]{3,1,0,2:T(8,128)(2,1)} %get-tuple-element.251, s32[]{:T(128)} %get-tuple-element.234), kind=kOutput, calls=%fused_computation.6.clone.1 | convolution fusion | flops 271579136 | bytes 5054976 | tf_op jit(solution)/shard_map/while/body/eval_jaxpr/qhgd,khd->hgqk/dot_general | solution.py:65
  316.6 3.3 fusion.60
  320.1 2.6 fusion.62
  (193 shorter events, 53.5 us)
Async XLA Ops:
  7.2 167.4 %copy-start = (bf16[1024,128]{1,0:T(8,128)(2,1)S(1)}, bf16[1024,128]{1,0:T(8,128)(2,1)}, u32[]{:S(2)}) copy-start(bf16[1024,128]{1,0:T(8,128)(2,1)} %param.18) | copy-start | bytes 786436
  7.2 225.6 %all-gather.3.cloned.1.call-start = ((), (), s32[]{:S(2)}) async-start(), calls=%async_computation.3 | async-start | bytes 2162688 | tf_op jit(solution)/shard_map/all_gather | solution.py:53
  16.3 15.5 %copy-start.4 = (bf16[192,1024]{1,0:T(8,128)(2,1)S(1)}, bf16[192,1024]{1,0:T(8,128)(2,1)}, u32[]{:S(2)}) copy-start(bf16[192,1024]{1,0:T(8,128)(2,1)} %param.21) | copy-start | bytes 1179652
  16.3 15.5 %copy-start.5 = (bf16[192,1024]{1,0:T(8,128)(2,1)S(1)}, bf16[192,1024]{1,0:T(8,128)(2,1)}, u32[]{:S(2)}) copy-start(bf16[192,1024]{1,0:T(8,128)(2,1)} %param.20) | copy-start | bytes 1179652
  17.9 13.9 %copy-start.6 = (bf16[192,1024]{1,0:T(8,128)(2,1)S(1)}, bf16[192,1024]{1,0:T(8,128)(2,1)}, u32[]{:S(2)}) copy-start(bf16[192,1024]{1,0:T(8,128)(2,1)} %param.19) | copy-start | bytes 1179652
  17.9 18.0 %copy-start.9 = (bf16[1,128,2,128]{3,2,1,0:T(2,128)(2,1)S(1)}, bf16[1,128,2,128]{3,2,1,0:T(2,128)(2,1)}, u32[]{:S(2)}) copy-start(bf16[1,128,2,128]{3,2,1,0:T(2,128)(2,1)} %param.15) | copy-start | bytes 196612
  17.9 41.9 %all-to-all-start = ((bf16[4,32,4,1024]{3,2,0,1:T(4,128)(2,1)}), bf16[4,32,4,1024]{3,2,0,1:T(4,128)(2,1)S(1)}, u32[]{:S(2)}, u32[]{:S(2)}) async-start(bf16[4,32,4,1024]{3,2,0,1:T(4,128)(2,1)} %copy.84), calls=%async_computation | async-start | bytes 2097152 | tf_op jit(solution)/shard_map/all_to_all | solution.py:137
  31.7 201.1 %all-gather.5.cloned.1.call-start = ((), (), s32[]{:S(2)}) async-start(), calls=%async_computation.4 | async-start | bytes 2162688 | tf_op jit(solution)/shard_map/all_gather | solution.py:54
  33.0 38.5 %collective-permute-start.15 = (bf16[3,192,1024]{2,1,0:T(8,128)(2,1)}, bf16[3,192,1024]{2,1,0:T(8,128)(2,1)}, u32[]{:S(2)}, u32[]{:S(2)}) collective-permute-start(bf16[3,192,1024]{2,1,0:T(8,128)(2,1)} %pad_maximum_fusion), channel_id=1, source_target_pairs={{0,1},{1,0},{2,3},{3,2},{4,5},{5,4},{6,7},{7,6},{8,9},{9,8},{10,11... | collective-permute-start | bytes 3538952 | tf_op jit(solution)/shard_map/ppermute | solution.py:25
  61.8 9.7 %copy-start.7 = (bf16[192,1024]{1,0:T(8,128)(2,1)S(1)}, bf16[192,1024]{1,0:T(8,128)(2,1)}, u32[]{:S(2)}) copy-start(bf16[192,1024]{1,0:T(8,128)(2,1)} %param.19) | copy-start | bytes 1179652
  63.2 20.5 %collective-permute-start = (bf16[1,16,4,1024]{3,2,1,0:T(4,128)(2,1)S(1)}, bf16[1,16,4,1024]{3,2,1,0:T(4,128)(2,1)S(1)}, u32[]{:S(2)}, u32[]{:S(2)}) collective-permute-start(bf16[1,16,4,1024]{3,2,1,0:T(4,128)(2,1)S(1)} %get-tuple-element.157), channel_id=1, source_target_pairs={{0,1},{1,0},{2,3},{3,2},{4,5},{5,4},{6,7},{7,6},{8,9},{9,8},{10,11... | collective-permute-start | bytes 393224 | tf_op jit(solution)/shard_map/ppermute | solution.py:19
  68.3 20.8 %collective-permute-start.1 = (bf16[1,16,4,1024]{3,2,1,0:T(4,128)(2,1)S(1)}, bf16[1,16,4,1024]{3,2,1,0:T(4,128)(2,1)S(1)}, u32[]{:S(2)}, u32[]{:S(2)}) collective-permute-start(bf16[1,16,4,1024]{3,2,1,0:T(4,128)(2,1)S(1)} %get-tuple-element.156), channel_id=1, source_target_pairs={{0,2},{1,3},{2,0},{3,1},{4,6},{5,7},{6,4},{7,5},{8,10},{9,11},{10,... | collective-permute-start | bytes 393224 | tf_op jit(solution)/shard_map/ppermute | solution.py:19
  74.9 16.3 %collective-permute-start.2 = (bf16[1,16,4,1024]{3,2,1,0:T(4,128)(2,1)S(1)}, bf16[1,16,4,1024]{3,2,1,0:T(4,128)(2,1)S(1)}, u32[]{:S(2)}, u32[]{:S(2)}) collective-permute-start(bf16[1,16,4,1024]{3,2,1,0:T(4,128)(2,1)S(1)} %get-tuple-element.155), channel_id=1, source_target_pairs={{0,3},{1,2},{2,1},{3,0},{4,7},{5,6},{6,5},{7,4},{8,11},{9,10},{10,... | collective-permute-start | bytes 393224 | tf_op jit(solution)/shard_map/ppermute | solution.py:19
  77.1 21.6 %collective-permute-start.3 = (bf16[1,16,4,1024]{3,2,1,0:T(4,128)(2,1)S(1)}, bf16[1,16,4,1024]{3,2,1,0:T(4,128)(2,1)S(1)}, u32[]{:S(2)}, u32[]{:S(2)}) collective-permute-start(bf16[1,16,4,1024]{3,2,1,0:T(4,128)(2,1)S(1)} %get-tuple-element.154), channel_id=1, source_target_pairs={{0,4},{1,5},{2,6},{3,7},{4,0},{5,1},{6,2},{7,3},{8,12},{9,13},{10,... | collective-permute-start | bytes 393224 | tf_op jit(solution)/shard_map/ppermute | solution.py:19
  81.3 23.5 %collective-permute-start.4 = (bf16[1,16,4,1024]{3,2,1,0:T(4,128)(2,1)S(1)}, bf16[1,16,4,1024]{3,2,1,0:T(4,128)(2,1)S(1)}, u32[]{:S(2)}, u32[]{:S(2)}) collective-permute-start(bf16[1,16,4,1024]{3,2,1,0:T(4,128)(2,1)S(1)} %get-tuple-element.153), channel_id=1, source_target_pairs={{0,5},{1,4},{2,7},{3,6},{4,1},{5,0},{6,3},{7,2},{8,13},{9,12},{10,... | collective-permute-start | bytes 393224 | tf_op jit(solution)/shard_map/ppermute | solution.py:19
  83.7 23.2 %collective-permute-start.5 = (bf16[1,16,4,1024]{3,2,1,0:T(4,128)(2,1)S(1)}, bf16[1,16,4,1024]{3,2,1,0:T(4,128)(2,1)S(1)}, u32[]{:S(2)}, u32[]{:S(2)}) collective-permute-start(bf16[1,16,4,1024]{3,2,1,0:T(4,128)(2,1)S(1)} %get-tuple-element.152), channel_id=1, source_target_pairs={{0,6},{1,7},{2,4},{3,5},{4,2},{5,3},{6,0},{7,1},{8,14},{9,15},{10,... | collective-permute-start | bytes 393224 | tf_op jit(solution)/shard_map/ppermute | solution.py:19
  89.1 34.5 %collective-permute-start.6 = (bf16[1,16,4,1024]{3,2,1,0:T(4,128)(2,1)S(1)}, bf16[1,16,4,1024]{3,2,1,0:T(4,128)(2,1)S(1)}, u32[]{:S(2)}, u32[]{:S(2)}) collective-permute-start(bf16[1,16,4,1024]{3,2,1,0:T(4,128)(2,1)S(1)} %get-tuple-element.151), channel_id=1, source_target_pairs={{0,7},{1,6},{2,5},{3,4},{4,3},{5,2},{6,1},{7,0},{8,15},{9,14},{10,... | collective-permute-start | bytes 393224 | tf_op jit(solution)/shard_map/ppermute | solution.py:19
  91.2 36.4 %collective-permute-start.7 = (bf16[1,16,4,1024]{3,2,1,0:T(4,128)(2,1)S(1)}, bf16[1,16,4,1024]{3,2,1,0:T(4,128)(2,1)S(1)}, u32[]{:S(2)}, u32[]{:S(2)}) collective-permute-start(bf16[1,16,4,1024]{3,2,1,0:T(4,128)(2,1)S(1)} %get-tuple-element.150), channel_id=1, source_target_pairs={{0,8},{1,9},{2,10},{3,11},{4,12},{5,13},{6,14},{7,15},{8,0},{9,1},... | collective-permute-start | bytes 393224 | tf_op jit(solution)/shard_map/ppermute | solution.py:19
  98.7 32.2 %collective-permute-start.8 = (bf16[1,16,4,1024]{3,2,1,0:T(4,128)(2,1)S(1)}, bf16[1,16,4,1024]{3,2,1,0:T(4,128)(2,1)S(1)}, u32[]{:S(2)}, u32[]{:S(2)}) collective-permute-start(bf16[1,16,4,1024]{3,2,1,0:T(4,128)(2,1)S(1)} %get-tuple-element.149), channel_id=1, source_target_pairs={{0,9},{1,8},{2,11},{3,10},{4,13},{5,12},{6,15},{7,14},{8,1},{9,0},... | collective-permute-start | bytes 393224 | tf_op jit(solution)/shard_map/ppermute | solution.py:19
  104.9 28.0 %collective-permute-start.9 = (bf16[1,16,4,1024]{3,2,1,0:T(4,128)(2,1)S(1)}, bf16[1,16,4,1024]{3,2,1,0:T(4,128)(2,1)S(1)}, u32[]{:S(2)}, u32[]{:S(2)}) collective-permute-start(bf16[1,16,4,1024]{3,2,1,0:T(4,128)(2,1)S(1)} %get-tuple-element.148), channel_id=1, source_target_pairs={{0,10},{1,11},{2,8},{3,9},{4,14},{5,15},{6,12},{7,13},{8,2},{9,3},... | collective-permute-start | bytes 393224 | tf_op jit(solution)/shard_map/ppermute | solution.py:19
  106.9 31.7 %collective-permute-start.10 = (bf16[1,16,4,1024]{3,2,1,0:T(4,128)(2,1)S(1)}, bf16[1,16,4,1024]{3,2,1,0:T(4,128)(2,1)S(1)}, u32[]{:S(2)}, u32[]{:S(2)}) collective-permute-start(bf16[1,16,4,1024]{3,2,1,0:T(4,128)(2,1)S(1)} %get-tuple-element.147), channel_id=1, source_target_pairs={{0,11},{1,10},{2,9},{3,8},{4,15},{5,14},{6,13},{7,12},{8,3},{9,2},... | collective-permute-start | bytes 393224 | tf_op jit(solution)/shard_map/ppermute | solution.py:19
  123.6 15.0 %collective-permute-start.11 = (bf16[1,16,4,1024]{3,2,1,0:T(4,128)(2,1)S(1)}, bf16[1,16,4,1024]{3,2,1,0:T(4,128)(2,1)S(1)}, u32[]{:S(2)}, u32[]{:S(2)}) collective-permute-start(bf16[1,16,4,1024]{3,2,1,0:T(4,128)(2,1)S(1)} %get-tuple-element.146), channel_id=1, source_target_pairs={{0,12},{1,13},{2,14},{3,15},{4,8},{5,9},{6,10},{7,11},{8,4},{9,5},... | collective-permute-start | bytes 393224 | tf_op jit(solution)/shard_map/ppermute | solution.py:19
  127.6 16.7 %collective-permute-start.12 = (bf16[1,16,4,1024]{3,2,1,0:T(4,128)(2,1)S(1)}, bf16[1,16,4,1024]{3,2,1,0:T(4,128)(2,1)S(1)}, u32[]{:S(2)}, u32[]{:S(2)}) collective-permute-start(bf16[1,16,4,1024]{3,2,1,0:T(4,128)(2,1)S(1)} %get-tuple-element.145), channel_id=1, source_target_pairs={{0,13},{1,12},{2,15},{3,14},{4,9},{5,8},{6,11},{7,10},{8,5},{9,4},... | collective-permute-start | bytes 393224 | tf_op jit(solution)/shard_map/ppermute | solution.py:19
  130.9 17.2 %collective-permute-start.13 = (bf16[1,16,4,1024]{3,2,1,0:T(4,128)(2,1)S(1)}, bf16[1,16,4,1024]{3,2,1,0:T(4,128)(2,1)S(1)}, u32[]{:S(2)}, u32[]{:S(2)}) collective-permute-start(bf16[1,16,4,1024]{3,2,1,0:T(4,128)(2,1)S(1)} %get-tuple-element.144), channel_id=1, source_target_pairs={{0,14},{1,15},{2,12},{3,13},{4,10},{5,11},{6,8},{7,9},{8,6},{9,7},... | collective-permute-start | bytes 393224 | tf_op jit(solution)/shard_map/ppermute | solution.py:19
  132.9 18.5 %collective-permute-start.14 = (bf16[1,16,4,1024]{3,2,1,0:T(4,128)(2,1)S(1)}, bf16[1,16,4,1024]{3,2,1,0:T(4,128)(2,1)S(1)}, u32[]{:S(2)}, u32[]{:S(2)}) collective-permute-start(bf16[1,16,4,1024]{3,2,1,0:T(4,128)(2,1)S(1)} %get-tuple-element.143), channel_id=1, source_target_pairs={{0,15},{1,14},{2,13},{3,12},{4,11},{5,10},{6,9},{7,8},{8,7},{9,6},... | collective-permute-start | bytes 393224 | tf_op jit(solution)/shard_map/ppermute | solution.py:19
  153.6 3.2 copy-start.2
  153.6 3.2 copy-start.3
  165.2 8.8 %copy-start.10 = (s32[1,128,2]{1,2,0:T(2,128)S(1)}, s32[1,128,2]{1,2,0:T(2,128)}, u32[]{:S(2)}) copy-start(s32[1,128,2]{1,2,0:T(2,128)} %param.16) | copy-start | bytes 3076
  165.3 57.6 %all-to-all-start.1 = ((bf16[16,16,4,1024]{3,1,2,0:T(8,128)(2,1)}), bf16[16,16,4,1024]{3,1,2,0:T(8,128)(2,1)S(1)}, u32[]{:S(2)}, u32[]{:S(2)}) async-start(bf16[16,16,4,1024]{3,1,2,0:T(8,128)(2,1)} %convolution_convert_fusion), calls=%async_computation.1 | async-start | bytes 4194304 | tf_op jit(solution)/shard_map/all_to_all | solution.py:155
  225.9 7.0 %copy-start.8 = (f32[2,8,128,128]{3,2,1,0:T(8,128)S(1)}, f32[2,8,128,128]{3,2,1,0:T(8,128)}, u32[]{:S(2)}) copy-start(f32[2,8,128,128]{3,2,1,0:T(8,128)} %custom-call.4) | copy-start | bytes 3145732
  227.7 96.6 %all-to-all-start.2 = ((bf16[4,32,4,1024]{3,2,0,1:T(4,128)(2,1)}), bf16[4,32,4,1024]{3,2,0,1:T(4,128)(2,1)S(1)}, u32[]{:S(2)}, u32[]{:S(2)}) async-start(bf16[4,32,4,1024]{3,2,0,1:T(4,128)(2,1)} %copy.88), calls=%async_computation.2 | async-start | bytes 2097152 | tf_op jit(solution)/shard_map/all_to_all | solution.py:162
  238.0 3.4 %copy-start.1 = (f32[2,512,128,8]{2,1,3,0:T(8,128)S(1)}, f32[2,512,128,8]{2,1,3,0:T(8,128)}, u32[]{:S(2)}) copy-start(f32[2,512,128,8]{2,1,3,0:T(8,128)} %get-tuple-element.219) | copy-start | bytes 12582916 | tf_op jit(solution)/shard_map/while
  249.2 3.4 %copy-start.1 = (f32[2,512,128,8]{2,1,3,0:T(8,128)S(1)}, f32[2,512,128,8]{2,1,3,0:T(8,128)}, u32[]{:S(2)}) copy-start(f32[2,512,128,8]{2,1,3,0:T(8,128)} %get-tuple-element.219) | copy-start | bytes 12582916 | tf_op jit(solution)/shard_map/while
  260.5 3.4 %copy-start.1 = (f32[2,512,128,8]{2,1,3,0:T(8,128)S(1)}, f32[2,512,128,8]{2,1,3,0:T(8,128)}, u32[]{:S(2)}) copy-start(f32[2,512,128,8]{2,1,3,0:T(8,128)} %get-tuple-element.219) | copy-start | bytes 12582916 | tf_op jit(solution)/shard_map/while
  271.7 3.4 %copy-start.1 = (f32[2,512,128,8]{2,1,3,0:T(8,128)S(1)}, f32[2,512,128,8]{2,1,3,0:T(8,128)}, u32[]{:S(2)}) copy-start(f32[2,512,128,8]{2,1,3,0:T(8,128)} %get-tuple-element.219) | copy-start | bytes 12582916 | tf_op jit(solution)/shard_map/while
  282.9 3.4 %copy-start.1 = (f32[2,512,128,8]{2,1,3,0:T(8,128)S(1)}, f32[2,512,128,8]{2,1,3,0:T(8,128)}, u32[]{:S(2)}) copy-start(f32[2,512,128,8]{2,1,3,0:T(8,128)} %get-tuple-element.219) | copy-start | bytes 12582916 | tf_op jit(solution)/shard_map/while
  294.2 3.4 %copy-start.1 = (f32[2,512,128,8]{2,1,3,0:T(8,128)S(1)}, f32[2,512,128,8]{2,1,3,0:T(8,128)}, u32[]{:S(2)}) copy-start(f32[2,512,128,8]{2,1,3,0:T(8,128)} %get-tuple-element.219) | copy-start | bytes 12582916 | tf_op jit(solution)/shard_map/while
  305.4 3.4 %copy-start.1 = (f32[2,512,128,8]{2,1,3,0:T(8,128)S(1)}, f32[2,512,128,8]{2,1,3,0:T(8,128)}, u32[]{:S(2)}) copy-start(f32[2,512,128,8]{2,1,3,0:T(8,128)} %get-tuple-element.219) | copy-start | bytes 12582916 | tf_op jit(solution)/shard_map/while
  316.6 3.4 %copy-start.1 = (f32[2,512,128,8]{2,1,3,0:T(8,128)S(1)}, f32[2,512,128,8]{2,1,3,0:T(8,128)}, u32[]{:S(2)}) copy-start(f32[2,512,128,8]{2,1,3,0:T(8,128)} %get-tuple-element.219) | copy-start | bytes 12582916 | tf_op jit(solution)/shard_map/while
Sparse Core Ops, SparseCore 0:
  11.8 87.4 all-gather.2
  103.0 80.6 all-gather.4
